TPU v7x, 512 devices: a whole 4x8x8 slice. The times are simulated.
512 devices in a mesh: section: 8 (over x, z_lo), dp: 64 (over y, z_hi, core).
Axes of the slice: x: 4, y: 8, z: 8 (z_hi: 4, z_lo: 2; z = z_hi * 2 + z_lo), core: 2. Of those that a mesh axis runs over, the one named last changes fastest.
Arguments:
- saved_input: bfloat16 [8, 256, 4096], P('section', 'dp'), may hold values from -6 to 6
- grad_sent: bfloat16 [8, 256, 4096], P('section', 'dp'), may hold values from -6 to 6
- kept_blocks: int32 [8, 1664], P('section', 'dp'), may hold values from 0 to 63, as said below
- gate_blocks: bfloat16 [8, 1664, 128, 128], P('section', 'dp'), may hold values from -0.15625 to 0.15625
- up_blocks: bfloat16 [8, 1664, 128, 128], P('section', 'dp'), may hold values from -0.15625 to 0.15625
- down_blocks: bfloat16 [8, 1664, 128, 128], P('section', 'dp'), may hold values from -0.078125 to 0.078125
Outputs:
- grad_input: bfloat16 [8, 256, 4096], P('section', 'dp')
- grad_gate: bfloat16 [8, 1664, 128, 128], P('section', 'dp')
- grad_up: bfloat16 [8, 1664, 128, 128], P('section', 'dp')
- grad_down: bfloat16 [8, 1664, 128, 128], P('section', 'dp')
Inputs may be any that keep to these rules, and one draw needn't show every extreme that they name: `kept_blocks`: each device's 26 ids are different and increasing; an id is the band along the model width times 2 plus the block among that device's hidden units; bands keep unequal shares of their blocks.
All inputs are finite; a program needn't handle non-finite values.
Results may differ from a plain program's by a relative error of at most 0.019.
Values may be sent and summed in bfloat16 or wider, within the bound.
No kernel may reach another device: no remote copies, remote signals or barrier semaphores. Data moves between devices by JAX's collectives and lax.ppermute only.
A program may use at most 64 MiB of HBM per device.

v0:
```python
import jax
import jax.numpy as jnp
from jax import lax
from jax.sharding import Mesh, PartitionSpec as P

FF = 16384
ROW_AXES = ("y", "zh", "core")


def passed_along(block, axis, distance):
    devices = range(lax.axis_size(axis))
    route = [((i - distance) % len(devices), i) for i in devices]
    return lax.ppermute(block, axis, route)


def shifted(block, axis, shift):
    n = lax.axis_size(axis)
    return lax.ppermute(block, axis, [(i, (i + shift) % n) for i in range(n)])


def shifted(block, axis, shift):
    n = lax.axis_size(axis)
    return lax.ppermute(block, axis, [(i, (i + shift) % n) for i in range(n)])


def gather_rows(block):
    for axis in (("y", "zh"), "core"):
        block = lax.all_gather(block, axis, axis=1, tiled=True)
    return block


def scatter_rows(block):
    for axis in ("core", "y"):
        block = lax.psum_scatter(block, axis, scatter_dimension=0, tiled=True)
    n = lax.axis_size("zh")
    idx = lax.axis_index("zh")
    chunks = jnp.split(block, n, axis=0)
    total = None
    for k in range(1, n):
        sent = jnp.stack(chunks)[(idx - k) % n]
        got = shifted(sent, "zh", -k)
        total = got if total is None else total + got
    return total + jnp.stack(chunks)[idx]


def per_device(saved_input, grad_sent, kept_blocks, gate_blocks, up_blocks, down_blocks):
    width = saved_input.shape[2]
    block = gate_blocks.shape[2]
    bands = width // block
    n_dp = 1
    for axis in ROW_AXES:
        n_dp *= lax.axis_size(axis)
    columns = FF // n_dp // block
    ids = kept_blocks[0]
    band_ids = ids // columns
    col_ids = ids % columns
    w_gate = gate_blocks[0]
    w_up = up_blocks[0]
    w_down = down_blocks[0]
    col_onehot = (col_ids[:, None] == jnp.arange(columns, dtype=jnp.int32)[None, :]).astype(
        jnp.float32
    )
    band_onehot = (band_ids[:, None] == jnp.arange(bands, dtype=jnp.int32)[None, :]).astype(
        jnp.float32
    )

    def to_columns(partial_value):
        spread = jnp.einsum("tkc,kn->tnc", partial_value, col_onehot)
        return spread.reshape(partial_value.shape[0], columns * block)

    def pick_cols(values):
        return jnp.take(values.reshape(values.shape[0], columns, block), col_ids, axis=1)

    def pick_bands(values):
        return jnp.take(values.reshape(values.shape[0], bands, block), band_ids, axis=1)

    incoming = passed_along(grad_sent, "section", -1)
    both = gather_rows(jnp.concatenate([saved_input, incoming], axis=0))
    inputs = both[0]
    upstream = both[1]
    chosen = pick_bands(inputs)
    gate = to_columns(
        jnp.einsum("tkb,kbc->tkc", chosen, w_gate, preferred_element_type=jnp.float32)
    )
    up = to_columns(jnp.einsum("tkb,kbc->tkc", chosen, w_up, preferred_element_type=jnp.float32))
    sig = jax.nn.sigmoid(gate)
    act = gate * sig
    hidden = (act * up).astype(jnp.bfloat16)
    grad_sel = pick_bands(upstream)
    dhid = to_columns(
        jnp.einsum("tkb,kcb->tkc", grad_sel, w_down, preferred_element_type=jnp.float32)
    )
    grad_up_act = (dhid * act).astype(jnp.bfloat16)
    grad_gate_act = (dhid * up * sig * (1.0 + gate * (1.0 - sig))).astype(jnp.bfloat16)
    input_sel = chosen
    tiles_down = jnp.einsum(
        "tkc,tkb->kcb", pick_cols(hidden), grad_sel, preferred_element_type=jnp.float32
    )
    tiles_gate = jnp.einsum(
        "tkb,tkc->kbc", input_sel, pick_cols(grad_gate_act), preferred_element_type=jnp.float32
    )
    tiles_up = jnp.einsum(
        "tkb,tkc->kbc", input_sel, pick_cols(grad_up_act), preferred_element_type=jnp.float32
    )
    slots = jnp.einsum(
        "tkc,kbc->tkb", pick_cols(grad_gate_act), w_gate, preferred_element_type=jnp.float32
    )
    slots = slots + jnp.einsum(
        "tkc,kbc->tkb", pick_cols(grad_up_act), w_up, preferred_element_type=jnp.float32
    )
    spread = jnp.einsum("tkb,kr->trb", slots, band_onehot)
    whole_term = spread.reshape(grad_gate_act.shape[0], bands * block)
    summed = scatter_rows(whole_term)
    grad_input = summed.astype(jnp.bfloat16)[None]
    return (
        grad_input,
        tiles_gate.astype(jnp.bfloat16)[None],
        tiles_up.astype(jnp.bfloat16)[None],
        tiles_down.astype(jnp.bfloat16)[None],
    )


def solution(mesh):
    n_dp = mesh.shape["dp"]
    split = Mesh(
        mesh.devices.reshape(mesh.shape["section"], n_dp // 8, 4, 2), ("section",) + ROW_AXES
    )
    rows = P("section", ROW_AXES, None)
    blocks = P("section", ROW_AXES, None, None)
    return jax.shard_map(
        per_device,
        mesh=split,
        in_specs=(rows, rows, P("section", ROW_AXES), blocks, blocks, blocks),
        out_specs=(rows, blocks, blocks, blocks),
        check_vma=False,
    )
```

profile of v0, /device:TPU:4, one launch (start us, length us, event | category | flops | bytes accessed | tf_op | source)
XLA Modules:
  0.0 264.7 jit_solution(5527434780666227582)
XLA Ops:
  7.2 4.4 %collective-permute-start = (bf16[1,4,4096]{2,1,0:T(4,128)(2,1)}, bf16[1,4,4096]{2,1,0:T(4,128)(2,1)S(1)}, u32[]{:S(2)}, u32[]{:S(2)}) collective-permute-start(bf16[1,4,4096]{2,1,0:T(4,128)(2,1)} %param.11), channel_id=1, source_target_pairs={{64,0},{128,64},{192,128},{256,192},{320,256},{384,320},{448,384},... | collective-permute-start | bytes 98312 | tf_op jit(solution)/shard_map/ppermute | solution.py:13
  11.6 2.1 collective-permute-done
  13.7 0.8 pad_maximum_fusion.1
  14.5 0.7 copy.47
  15.3 93.7 %all-gather.3.cloned.1.call-done = bf16[2,128,4096]{2,0,1:T(2,128)(2,1)} async-done(((bf16[2,4,4096]{2,0,1:T(2,128)(2,1)}), bf16[2,128,4096]{2,0,1:T(2,128)(2,1)}) %all-gather.3.cloned.1.call-update) | async-done | bytes 2097168 | tf_op jit(solution)/shard_map/all_gather | solution.py:28
  109.0 6.2 %copy.48 = bf16[2,128,4096]{1,2,0:T(8,128)(2,1)} copy(bf16[2,128,4096]{2,0,1:T(2,128)(2,1)} %all-gather.3.cloned.1.call-done) | data formatting | bytes 4194304 | tf_op jit(solution)/shard_map/all_gather | solution.py:28
  115.9 16.1 %all-gather.5.cloned.1.call-done = bf16[2,256,4096]{1,2,0:T(8,128)(2,1)} async-done(((bf16[2,128,4096]{1,2,0:T(8,128)(2,1)}), bf16[2,256,4096]{1,2,0:T(8,128)(2,1)}) %all-gather.5.cloned.1.call-update) | async-done | bytes 4194320 | tf_op jit(solution)/shard_map/all_gather | solution.py:28
  132.0 4.5 %fusion.87 = (bf16[1,256,4096]{1,2,0:T(8,128)(2,1)}, bf16[1,256,4096]{1,2,0:T(8,128)(2,1)}) fusion(bf16[2,256,4096]{1,2,0:T(8,128)(2,1)} %all-gather.5.cloned.1.call-done), kind=kLoop, calls=%fused_computation.106 | loop fusion | bytes 8388608 | tf_op jit(solution)/shard_map/slice | solution.py:80
  136.5 3.2 %copy.49 = bf16[256,32,128]{2,0,1:T(8,128)(2,1)S(1)} copy(bf16[256,32,128]{0,2,1:T(8,128)(2,1)} %bitcast.175) | data formatting | bytes 4194304 | tf_op jit(solution)/shard_map/reshape;squeeze | solution.py:75
  139.7 4.1 %copy.52 = bf16[256,32,128]{2,0,1:T(8,128)(2,1)} copy(bf16[256,32,128]{0,2,1:T(8,128)(2,1)} %bitcast.174) | data formatting | bytes 4194304 | tf_op jit(solution)/shard_map/reshape;squeeze | solution.py:75
  143.8 2.0 gather_fusion
  145.8 2.5 gather_fusion.1
  148.2 0.7 convolution_bitcast_fusion
  148.9 1.1 fusion.2
  150.1 0.7 convolution_bitcast_fusion.1
  150.7 1.1 fusion.4
  152.9 1.1 fusion.6
  154.1 0.9 gather_fusion.2
  155.0 2.0 gather_fusion.3
  157.7 0.8 copy-done.1
  159.3 1.1 fusion
  160.5 5.9 %copy.84 = f32[32,8,32,128]{3,1,2,0:T(8,128)} copy(f32[32,8,32,128]{3,2,1,0:T(8,128)S(1)} %bitcast.173) | data formatting | bytes 8388608
  166.5 21.7 %reduce-scatter.3.cloned.1.call-done = f32[128,4096]{1,0:T(8,128)} async-done(((f32[256,4096]{1,0:T(8,128)}), f32[128,4096]{1,0:T(8,128)}) %reduce-scatter.3.cloned.1.call-update) | async-done | bytes 2097168 | tf_op jit(solution)/shard_map/reduce_scatter | solution.py:34
  188.3 2.0 gather_fusion.4
  190.3 3.3 %fusion.50 = bf16[1,26,128,128]{3,2,1,0:T(8,128)(2,1)} fusion(bf16[26,256,128]{2,1,0:T(8,128)(2,1)S(1)} %gather_fusion.2, pred[26]{0:T(512)(128)(4,1)S(1)} %get-tuple-element.6, bf16[26,256,128]{2,1,0:T(8,128)(2,1)} %copy-done.5, pred[26]{0:T(512)(128)(4,1)S(1)} %get-tuple-element.22), kind=kOutput, calls=%fused_computation.44 | convolution fusion | flops 220233728 | bytes 4259892 | tf_op jit(solution)/shard_map/tkb,tkc->kbc/dot_general | solution.py:99
  193.6 1.7 fusion.45
  195.4 41.3 %reduce-scatter.5.cloned.1.call-done = f32[16,4096]{1,0:T(8,128)} async-done(((f32[128,4096]{1,0:T(8,128)}), f32[16,4096]{1,0:T(8,128)}) %reduce-scatter.5.cloned.1.call-update) | async-done | bytes 262160 | tf_op jit(solution)/shard_map/reduce_scatter | solution.py:34
  236.6 1.1 slice_bitcast_fusion.3
  237.9 8.5 %collective-permute-start.2 = (f32[4,4096]{1,0:T(4,128)S(1)}, f32[4,4096]{1,0:T(4,128)S(1)}, u32[]{:S(2)}, u32[]{:S(2)}) collective-permute-start(f32[4,4096]{1,0:T(4,128)S(1)} %get-tuple-element.15), channel_id=1, source_target_pairs={{0,4},{2,6},{4,0},{6,2},{1,5},{3,7},{5,1},{7,3},{8,12},{10,14},{12... | collective-permute-start | bytes 196616 | tf_op jit(solution)/shard_map/ppermute | solution.py:23
  246.4 2.4 collective-permute-start.3
  248.8 5.5 %collective-permute-start.1 = (f32[4,4096]{1,0:T(4,128)S(1)}, f32[4,4096]{1,0:T(4,128)S(1)}, u32[]{:S(2)}, u32[]{:S(2)}) collective-permute-start(f32[4,4096]{1,0:T(4,128)S(1)} %get-tuple-element.17), channel_id=1, source_target_pairs={{0,6},{2,0},{4,2},{6,4},{1,7},{3,1},{5,3},{7,5},{8,14},{10,8},{12,... | collective-permute-start | bytes 196616 | tf_op jit(solution)/shard_map/ppermute | solution.py:23
  254.4 3.2 %fusion.40 = bf16[1,26,128,128]{3,2,1,0:T(8,128)(2,1)} fusion(bf16[26,256,128]{2,1,0:T(8,128)(2,1)} %gather_fusion.4, pred[26]{0:T(512)(128)(4,1)S(1)} %get-tuple-element.6, bf16[26,256,128]{2,1,0:T(8,128)(2,1)S(1)} %copy-done.4, pred[26]{0:T(512)(128)(4,1)S(1)} %get-tuple-element.22), kind=kOutput, calls=%fused_computation.42 | convolution fusion | flops 220233728 | bytes 4259892 | tf_op jit(solution)/shard_map/tkc,tkb->kcb/dot_general | solution.py:96
  (43 shorter events, 4.5 us)
Async XLA Ops:
  7.2 141.1 %copy-start = (bf16[1,26,128,128]{3,2,1,0:T(8,128)(2,1)S(1)}, bf16[1,26,128,128]{3,2,1,0:T(8,128)(2,1)}, u32[]{:S(2)}) copy-start(bf16[1,26,128,128]{3,2,1,0:T(8,128)(2,1)} %param.13) | copy-start | bytes 2555908
  7.2 101.9 %all-gather.3.cloned.1.call-start = ((), (), s32[]{:S(2)}) async-start(), calls=%async_computation.2 | async-start | bytes 2162688 | tf_op jit(solution)/shard_map/all_gather | solution.py:28
  7.2 6.5 %collective-permute-start = (bf16[1,4,4096]{2,1,0:T(4,128)(2,1)}, bf16[1,4,4096]{2,1,0:T(4,128)(2,1)S(1)}, u32[]{:S(2)}, u32[]{:S(2)}) collective-permute-start(bf16[1,4,4096]{2,1,0:T(4,128)(2,1)} %param.11), channel_id=1, source_target_pairs={{64,0},{128,64},{192,128},{256,192},{320,256},{384,320},{448,384},... | collective-permute-start | bytes 98312 | tf_op jit(solution)/shard_map/ppermute | solution.py:13
  15.3 116.7 %all-gather.5.cloned.1.call-start = ((), (), s32[]{:S(2)}) async-start(), calls=%async_computation.3 | async-start | bytes 6291456 | tf_op jit(solution)/shard_map/all_gather | solution.py:28
  115.2 0.7 copy-start.9
  115.2 72.9 %reduce-scatter.3.cloned.1.call-start = ((), (), s32[]{:S(2)}) async-start(), calls=%async_computation.4 | async-start | bytes 6291456 | tf_op jit(solution)/shard_map/reduce_scatter | solution.py:34
  148.2 1.7 copy-start.5
  148.9 1.2 copy-start.7
  150.1 1.7 copy-start.10
  150.7 1.5 copy-start.3
  157.0 1.5 copy-start.1
  157.0 1.7 copy-start.8
  166.4 70.2 %reduce-scatter.5.cloned.1.call-start = ((), (), s32[]{:S(2)}) async-start(), calls=%async_computation.5 | async-start | bytes 2359296 | tf_op jit(solution)/shard_map/reduce_scatter | solution.py:34
  190.3 3.3 %copy-start.2 = (bf16[26,256,128]{2,1,0:T(8,128)(2,1)S(1)}, bf16[26,256,128]{2,1,0:T(8,128)(2,1)}, u32[]{:S(2)}) copy-start(bf16[26,256,128]{2,1,0:T(8,128)(2,1)} %gather_fusion.3) | copy-start | bytes 5111812
  190.3 3.3 %copy-start.6 = (bf16[26,256,128]{2,1,0:T(8,128)(2,1)S(1)}, bf16[26,256,128]{2,1,0:T(8,128)(2,1)}, u32[]{:S(2)}) copy-start(bf16[26,256,128]{2,1,0:T(8,128)(2,1)} %copy-done.5) | copy-start | bytes 5111812
  193.6 60.7 %copy-start.4 = (bf16[26,256,128]{2,1,0:T(8,128)(2,1)S(1)}, bf16[26,256,128]{2,1,0:T(8,128)(2,1)}, u32[]{:S(2)}) copy-start(bf16[26,256,128]{2,1,0:T(8,128)(2,1)} %gather_fusion) | copy-start | bytes 5111812
  237.9 19.7 %collective-permute-start.2 = (f32[4,4096]{1,0:T(4,128)S(1)}, f32[4,4096]{1,0:T(4,128)S(1)}, u32[]{:S(2)}, u32[]{:S(2)}) collective-permute-start(f32[4,4096]{1,0:T(4,128)S(1)} %get-tuple-element.15), channel_id=1, source_target_pairs={{0,4},{2,6},{4,0},{6,2},{1,5},{3,7},{5,1},{7,3},{8,12},{10,14},{12... | collective-permute-start | bytes 196616 | tf_op jit(solution)/shard_map/ppermute | solution.py:23
  246.4 11.2 %collective-permute-start.3 = (f32[4,4096]{1,0:T(4,128)S(1)}, f32[4,4096]{1,0:T(4,128)S(1)}, u32[]{:S(2)}, u32[]{:S(2)}) collective-permute-start(f32[4,4096]{1,0:T(4,128)S(1)} %get-tuple-element.16), channel_id=1, source_target_pairs={{0,2},{2,4},{4,6},{6,0},{1,3},{3,5},{5,7},{7,1},{8,10},{10,12},{12... | collective-permute-start | bytes 196616 | tf_op jit(solution)/shard_map/ppermute | solution.py:23
  248.8 8.7 %collective-permute-start.1 = (f32[4,4096]{1,0:T(4,128)S(1)}, f32[4,4096]{1,0:T(4,128)S(1)}, u32[]{:S(2)}, u32[]{:S(2)}) collective-permute-start(f32[4,4096]{1,0:T(4,128)S(1)} %get-tuple-element.17), channel_id=1, source_target_pairs={{0,6},{2,0},{4,2},{6,4},{1,7},{3,1},{5,3},{7,5},{8,14},{10,8},{12,... | collective-permute-start | bytes 196616 | tf_op jit(solution)/shard_map/ppermute | solution.py:23
Sparse Core Ops, SparseCore 0:
  15.4 93.6 all-gather.2
  115.3 16.5 all-gather.4
  166.5 21.5 reduce-scatter.2
  191.1 45.4 reduce-scatter.4
where the time goes:
time: 265 us
  waiting for transfers between devices  175 us (66%)
  local copies, waits for them, and re-layouts  37.3 us (14%)
  starting transfers between devices  21 us (8%)
  matrix products  15.8 us (6%)
  between operations  14 us (5%)
    all_gather x2, waiting for transfers between devices, gather_rows(): block = lax.all_gather(block, axis, axis=1, tiled=True)  110 us
    reduce_scatter x2, waiting for transfers between devices, scatter_rows(): block = lax.psum_scatter(block, axis, scatter_dimension=0, tiled=True)  63 us
    ppermute x3, starting transfers between devices, shifted(): return lax.ppermute(block, axis, [(i, (i + shift) % n) for i in range(n)])  16.5 us
    unnamed x23, local copies, waits for them, and re-layouts  8.1 us
    another operation x2, local copies, waits for them, and re-layouts, pick_bands(): values.reshape(values.shape[0], bands, block)  7.28 us
    all_gather x1, local copies, waits for them, and re-layouts, gather_rows(): block = lax.all_gather(block, axis, axis=1, tiled=True)  6.16 us
  transfers between devices with their start and end apart: 8, of which 5 were waited for; matrix products, arithmetic and copies ran while one was open for 4% of the time, Pallas kernels for 0%

commit v1 on v0

--- a/solution.py
+++ b/solution.py
@@ -5,6 +5,9 @@
 
 FF = 16384
 ROW_AXES = ("y", "zh", "core")
+_use_lanes = lambda piece_in, mesh_ax: jnp.concatenate(
+    lax.all_to_all(jnp.stack([piece_in] * lax.axis_size(mesh_ax), 0), mesh_ax, 0, 0), 1
+)
 
 
 def passed_along(block, axis, distance):
@@ -25,7 +28,7 @@
 
 def gather_rows(block):
     for axis in (("y", "zh"), "core"):
-        block = lax.all_gather(block, axis, axis=1, tiled=True)
+        block = _use_lanes(block, axis)
     return block
 
 

time: 265 us -> 248 us (0.936)
  the two profiles are of different devices: /device:TPU:4 before, /device:TPU:2 now
where the time goes in v1:
time: 248 us
  waiting for transfers between devices  117 us (47%)
  local copies, waits for them, and re-layouts  47.5 us (19%)
  starting transfers between devices  36.8 us (15%)
  matrix products  15.8 us (6%)
  between operations  14.4 us (6%)
  blocking collectives  8.48 us (3%)
  other arithmetic  7.45 us (3%)
    reduce_scatter x2, waiting for transfers between devices, scatter_rows(): block = lax.psum_scatter(block, axis, scatter_dimension=0, tiled=True)  62.7 us
    all_to_all x1, waiting for transfers between devices, lax.all_to_all(jnp.stack([piece_in] * lax.axis_size(mesh_ax), 0), mesh_ax...  52.5 us
    slice x1, local copies, waits for them, and re-layouts, per_device(): upstream = both[1]  21.3 us
    ppermute x3, starting transfers between devices, shifted(): return lax.ppermute(block, axis, [(i, (i + shift) % n) for i in range(n)])  16.6 us
    all_to_all x1, starting transfers between devices, lax.all_to_all(jnp.stack([piece_in] * lax.axis_size(mesh_ax), 0), mesh_ax...  15.7 us
    unnamed x27, local copies, waits for them, and re-layouts  9.29 us
    all_to_all x1, blocking collectives, lax.all_to_all(jnp.stack([piece_in] * lax.axis_size(mesh_ax), 0), mesh_ax...  8.48 us
    another operation x1, other arithmetic, jnp.stack([piece_in] * lax.axis_size(mesh_ax), 0)  5.73 us
  transfers between devices with their start and end apart: 7, of which 4 were waited for; matrix products, arithmetic and copies ran while one was open for 4% of the time, Pallas kernels for 0%

profile of v1, /device:TPU:2, one launch (start us, length us, event | category | flops | bytes accessed | tf_op | source)
XLA Modules:
  0.0 247.8 jit_solution(10372976451052880842)
XLA Ops:
  7.2 4.4 %collective-permute-start = (bf16[1,4,4096]{2,1,0:T(4,128)(2,1)}, bf16[1,4,4096]{2,1,0:T(4,128)(2,1)S(1)}, u32[]{:S(2)}, u32[]{:S(2)}) collective-permute-start(bf16[1,4,4096]{2,1,0:T(4,128)(2,1)} %param.11), channel_id=1, source_target_pairs={{64,0},{128,64},{192,128},{256,192},{320,256},{384,320},{448,384},... | collective-permute-start | bytes 98312 | tf_op jit(solution)/shard_map/ppermute | solution.py:16
  11.6 2.1 collective-permute-done
  13.7 0.8 pad_maximum_fusion.2
  14.6 3.4 %stack.14 = bf16[32,2,4,4096]{3,1,2,0:T(2,128)(2,1)} broadcast(bf16[2,4,4096]{2,0,1:T(2,128)(2,1)S(1)} %copy.33), dimensions={1,2,3} | broadcast | bytes 2162688 | tf_op jit(solution)/shard_map/stack | solution.py:9
  18.0 15.7 %all-to-all-start = ((bf16[32,2,4,4096]{3,1,2,0:T(2,128)(2,1)}), bf16[32,2,4,4096]{3,1,2,0:T(2,128)(2,1)S(1)}, u32[]{:S(2)}, u32[]{:S(2)}) async-start(bf16[32,2,4,4096]{3,1,2,0:T(2,128)(2,1)} %stack.14), calls=%async_computation | async-start | bytes 4194304 | tf_op jit(solution)/shard_map/all_to_all | solution.py:9
  33.9 52.5 %all-to-all-done = bf16[32,2,4,4096]{3,1,2,0:T(2,128)(2,1)S(1)} async-done(((bf16[32,2,4,4096]{3,1,2,0:T(2,128)(2,1)}), bf16[32,2,4,4096]{3,1,2,0:T(2,128)(2,1)S(1)}, u32[]{:S(2)}, u32[]{:S(2)}) %all-to-all-start) | async-done | bytes 2097184 | tf_op jit(solution)/shard_map/all_to_all | solution.py:9
  86.4 5.7 %pad_maximum_fusion = bf16[2,2,128,4096]{3,1,2,0:T(2,128)(2,1)} fusion(bf16[1,2,128,4096]{3,1,2,0:T(2,128)(2,1)S(1)} %bitcast.183), kind=kLoop, calls=%fused_computation.8 | loop fusion | flops 2097152 | bytes 6291456 | tf_op jit(solution)/shard_map/stack | solution.py:9
  92.1 8.5 %all_to_all.10 = bf16[2,2,128,4096]{3,1,2,0:T(2,128)(2,1)S(1)} all-to-all(bf16[2,2,128,4096]{3,1,2,0:T(2,128)(2,1)} %pad_maximum_fusion), channel_id=1, replica_groups=mesh['section'=8,'y'=8,'zh'=4,'core'=2] {'core'}, dimensions={0} | all-to-all | bytes 8388608 | tf_op jit(solution)/shard_map/all_to_all | solution.py:9
  100.6 21.3 %slice_reduce_fusion.1 = (bf16[2,128,4096]{2,1,0:T(8,128)(2,1)S(1)}, bf16[2,128,4096]{2,1,0:T(8,128)(2,1)}) fusion(bf16[2,2,128,4096]{3,0,2,1:T(2,128)(2,1)S(1)} %bitcast.180), kind=kLoop, calls=%fused_computation.7 | loop fusion | bytes 8388608 | tf_op jit(solution)/shard_map/slice | solution.py:83
  122.3 0.8 copy.34
  123.2 0.8 copy-done.3
  124.4 2.2 copy.37
  126.6 2.0 gather_fusion
  128.6 2.5 gather_fusion.1
  131.7 1.1 fusion.2
  133.6 1.1 fusion.4
  135.7 1.1 fusion.6
  137.0 0.9 gather_fusion.2
  137.8 2.0 gather_fusion.3
  140.5 0.8 copy-done.1
  142.2 1.1 fusion
  143.3 6.0 %copy.71 = f32[32,8,32,128]{3,1,2,0:T(8,128)} copy(f32[32,8,32,128]{3,2,1,0:T(8,128)S(1)} %bitcast.182) | data formatting | bytes 8388608
  149.3 21.3 %reduce-scatter.3.cloned.1.call-done = f32[128,4096]{1,0:T(8,128)} async-done(((f32[256,4096]{1,0:T(8,128)}), f32[128,4096]{1,0:T(8,128)}) %reduce-scatter.3.cloned.1.call-update) | async-done | bytes 2097168 | tf_op jit(solution)/shard_map/reduce_scatter | solution.py:37
  170.8 2.0 gather_fusion.4
  172.8 3.3 %fusion.50 = bf16[1,26,128,128]{3,2,1,0:T(8,128)(2,1)} fusion(bf16[26,256,128]{2,1,0:T(8,128)(2,1)S(1)} %gather_fusion.2, pred[26]{0:T(512)(128)(4,1)S(1)} %get-tuple-element.8, bf16[26,256,128]{2,1,0:T(8,128)(2,1)} %copy-done.6, pred[26]{0:T(512)(128)(4,1)S(1)} %get-tuple-element.22), kind=kOutput, calls=%fused_computation.47 | convolution fusion | flops 220233728 | bytes 4259892 | tf_op jit(solution)/shard_map/tkb,tkc->kbc/dot_general | solution.py:102
  176.1 1.7 fusion.45
  177.8 41.4 %reduce-scatter.5.cloned.1.call-done = f32[16,4096]{1,0:T(8,128)} async-done(((f32[128,4096]{1,0:T(8,128)}), f32[16,4096]{1,0:T(8,128)}) %reduce-scatter.5.cloned.1.call-update) | async-done | bytes 262160 | tf_op jit(solution)/shard_map/reduce_scatter | solution.py:37
  219.2 1.1 slice_bitcast_fusion.3
  220.4 8.7 %collective-permute-start.2 = (f32[4,4096]{1,0:T(4,128)S(1)}, f32[4,4096]{1,0:T(4,128)S(1)}, u32[]{:S(2)}, u32[]{:S(2)}) collective-permute-start(f32[4,4096]{1,0:T(4,128)S(1)} %get-tuple-element.15), channel_id=1, source_target_pairs={{0,4},{2,6},{4,0},{6,2},{1,5},{3,7},{5,1},{7,3},{8,12},{10,14},{12... | collective-permute-start | bytes 196616 | tf_op jit(solution)/shard_map/ppermute | solution.py:26
  229.1 2.3 collective-permute-start.3
  231.4 5.7 %collective-permute-start.1 = (f32[4,4096]{1,0:T(4,128)S(1)}, f32[4,4096]{1,0:T(4,128)S(1)}, u32[]{:S(2)}, u32[]{:S(2)}) collective-permute-start(f32[4,4096]{1,0:T(4,128)S(1)} %get-tuple-element.17), channel_id=1, source_target_pairs={{0,6},{2,0},{4,2},{6,4},{1,7},{3,1},{5,3},{7,5},{8,14},{10,8},{12,... | collective-permute-start | bytes 196616 | tf_op jit(solution)/shard_map/ppermute | solution.py:26
  237.1 3.2 %fusion.40 = bf16[1,26,128,128]{3,2,1,0:T(8,128)(2,1)} fusion(bf16[26,256,128]{2,1,0:T(8,128)(2,1)} %gather_fusion.4, pred[26]{0:T(512)(128)(4,1)S(1)} %get-tuple-element.8, bf16[26,256,128]{2,1,0:T(8,128)(2,1)S(1)} %copy-done.5, pred[26]{0:T(512)(128)(4,1)S(1)} %get-tuple-element.22), kind=kOutput, calls=%fused_computation.45 | convolution fusion | flops 220233728 | bytes 4259892 | tf_op jit(solution)/shard_map/tkc,tkb->kcb/dot_general | solution.py:99
  (45 shorter events, 6.2 us)
Async XLA Ops:
  7.2 123.9 %copy-start = (bf16[1,26,128,128]{3,2,1,0:T(8,128)(2,1)S(1)}, bf16[1,26,128,128]{3,2,1,0:T(8,128)(2,1)}, u32[]{:S(2)}) copy-start(bf16[1,26,128,128]{3,2,1,0:T(8,128)(2,1)} %param.13) | copy-start | bytes 2555908
  7.2 6.5 %collective-permute-start = (bf16[1,4,4096]{2,1,0:T(4,128)(2,1)}, bf16[1,4,4096]{2,1,0:T(4,128)(2,1)S(1)}, u32[]{:S(2)}, u32[]{:S(2)}) collective-permute-start(bf16[1,4,4096]{2,1,0:T(4,128)(2,1)} %param.11), channel_id=1, source_target_pairs={{64,0},{128,64},{192,128},{256,192},{320,256},{384,320},{448,384},... | collective-permute-start | bytes 98312 | tf_op jit(solution)/shard_map/ppermute | solution.py:16
  18.0 15.8 %copy-start.10 = (s32[1,26]{1,0:T(1,128)S(1)}, s32[1,26]{1,0:T(1,128)}, u32[]{:S(2)}) copy-start(s32[1,26]{1,0:T(1,128)} %param.12) | copy-start | bytes 316
  18.0 68.4 %all-to-all-start = ((bf16[32,2,4,4096]{3,1,2,0:T(2,128)(2,1)}), bf16[32,2,4,4096]{3,1,2,0:T(2,128)(2,1)S(1)}, u32[]{:S(2)}, u32[]{:S(2)}) async-start(bf16[32,2,4,4096]{3,1,2,0:T(2,128)(2,1)} %stack.14), calls=%async_computation | async-start | bytes 4194304 | tf_op jit(solution)/shard_map/all_to_all | solution.py:9
  33.7 136.9 %reduce-scatter.3.cloned.1.call-start = ((), (), s32[]{:S(2)}) async-start(), calls=%async_computation.4 | async-start | bytes 6291456 | tf_op jit(solution)/shard_map/reduce_scatter | solution.py:37
  122.3 1.6 copy-start.3
  131.0 2.5 %copy-start.6 = (bf16[26,256,128]{2,1,0:T(8,128)(2,1)}, bf16[26,256,128]{2,1,0:T(8,128)(2,1)S(1)}, u32[]{:S(2)}) copy-start(bf16[26,256,128]{2,1,0:T(8,128)(2,1)S(1)} %gather_fusion.1) | copy-start | bytes 5111812
  131.7 1.2 copy-start.8
  132.9 1.7 copy-start.11
  133.6 1.5 copy-start.4
  139.8 1.5 copy-start.1
  139.8 1.7 copy-start.9
  149.3 69.9 %reduce-scatter.5.cloned.1.call-start = ((), (), s32[]{:S(2)}) async-start(), calls=%async_computation.5 | async-start | bytes 2359296 | tf_op jit(solution)/shard_map/reduce_scatter | solution.py:37
  172.8 3.3 %copy-start.2 = (bf16[26,256,128]{2,1,0:T(8,128)(2,1)S(1)}, bf16[26,256,128]{2,1,0:T(8,128)(2,1)}, u32[]{:S(2)}) copy-start(bf16[26,256,128]{2,1,0:T(8,128)(2,1)} %gather_fusion.3) | copy-start | bytes 5111812
  172.8 3.3 %copy-start.7 = (bf16[26,256,128]{2,1,0:T(8,128)(2,1)S(1)}, bf16[26,256,128]{2,1,0:T(8,128)(2,1)}, u32[]{:S(2)}) copy-start(bf16[26,256,128]{2,1,0:T(8,128)(2,1)} %copy-done.6) | copy-start | bytes 5111812
  176.1 61.0 %copy-start.5 = (bf16[26,256,128]{2,1,0:T(8,128)(2,1)S(1)}, bf16[26,256,128]{2,1,0:T(8,128)(2,1)}, u32[]{:S(2)}) copy-start(bf16[26,256,128]{2,1,0:T(8,128)(2,1)} %gather_fusion) | copy-start | bytes 5111812
  220.4 19.8 %collective-permute-start.2 = (f32[4,4096]{1,0:T(4,128)S(1)}, f32[4,4096]{1,0:T(4,128)S(1)}, u32[]{:S(2)}, u32[]{:S(2)}) collective-permute-start(f32[4,4096]{1,0:T(4,128)S(1)} %get-tuple-element.15), channel_id=1, source_target_pairs={{0,4},{2,6},{4,0},{6,2},{1,5},{3,7},{5,1},{7,3},{8,12},{10,14},{12... | collective-permute-start | bytes 196616 | tf_op jit(solution)/shard_map/ppermute | solution.py:26
  229.1 11.2 %collective-permute-start.3 = (f32[4,4096]{1,0:T(4,128)S(1)}, f32[4,4096]{1,0:T(4,128)S(1)}, u32[]{:S(2)}, u32[]{:S(2)}) collective-permute-start(f32[4,4096]{1,0:T(4,128)S(1)} %get-tuple-element.16), channel_id=1, source_target_pairs={{0,2},{2,4},{4,6},{6,0},{1,3},{3,5},{5,7},{7,1},{8,10},{10,12},{12... | collective-permute-start | bytes 196616 | tf_op jit(solution)/shard_map/ppermute | solution.py:26
  231.4 8.8 %collective-permute-start.1 = (f32[4,4096]{1,0:T(4,128)S(1)}, f32[4,4096]{1,0:T(4,128)S(1)}, u32[]{:S(2)}, u32[]{:S(2)}) collective-permute-start(f32[4,4096]{1,0:T(4,128)S(1)} %get-tuple-element.17), channel_id=1, source_target_pairs={{0,6},{2,0},{4,2},{6,4},{1,7},{3,1},{5,3},{7,5},{8,14},{10,8},{12,... | collective-permute-start | bytes 196616 | tf_op jit(solution)/shard_map/ppermute | solution.py:26
Sparse Core Ops, SparseCore 0:
  149.4 21.2 reduce-scatter.2
  173.7 45.4 reduce-scatter.4
